TPU v7x, 128 devices: a whole 4x4x4 slice. The times are simulated.
128 devices in a mesh: row: 8 (over x_lo, z), col: 16 (over y, x_hi, core).
Axes of the slice: x: 4 (x_hi: 2, x_lo: 2; x = x_hi * 2 + x_lo), y: 4, z: 4, core: 2. Of those that a mesh axis runs over, the one named last changes fastest.
Arguments:
- adjusted_rows: bfloat16 [8192, 29568], P(('row', 'col')), may hold values from -5 to 5
- base_weight: bfloat16 [8192, 29568], P('row', 'col'), may hold values from -5 to 5
- range_test: bfloat16 [29568, 384], P('col'), may hold values from -0.03125 to 0.03125
- corange_test: bfloat16 [384, 8192], P(None, 'row'), may hold values from -0.0625 to 0.0625
- core_left: bfloat16 [768, 8192], P(None, 'row'), may hold values from -0.0625 to 0.0625
- core_right: bfloat16 [768, 29568], P(None, 'col'), may hold values from -1 to 1
Outputs:
- range_sketch: float32 [8192, 384], P('row')
- corange_sketch: float32 [384, 29568], P(None, 'col')
- core_solution: float32 [384, 768], P(None, 'col')
All inputs are finite; a program needn't handle non-finite values.
Results may differ from a plain program's by a relative error of at most 0.0066.
Values may be sent and summed in bfloat16 or wider, within the bound.
No kernel may reach another device: no remote copies, remote signals or barrier semaphores. Data moves between devices by JAX's collectives and lax.ppermute only.
A program may use at most 128 MiB of HBM per device.

v0:
```python
import jax
import jax.numpy as jnp
from jax import lax
from jax.sharding import PartitionSpec as P

S = 768


def scatter_sum(part, axis, groups):
    rows = part.shape[0] // groups
    got = lax.all_to_all(part, axis, split_axis=0, concat_axis=0, tiled=True)
    return got.reshape(groups, rows, *part.shape[1:]).sum(axis=0)


def gather_rows(chunk, axis, groups):
    tiled = jnp.broadcast_to(chunk[None], (groups, *chunk.shape)).reshape(
        groups * chunk.shape[0], *chunk.shape[1:]
    )
    return lax.all_to_all(tiled, axis, split_axis=0, concat_axis=0, tiled=True)


def local(adjusted_rows, base_weight, range_test, corange_test, core_left, core_right):
    highest = lax.Precision.HIGHEST
    ncol = lax.axis_size("col")
    nrow = lax.axis_size("row")
    height, width = adjusted_rows.shape[0], adjusted_rows.shape[1] // ncol
    by_target = adjusted_rows.reshape(height, ncol, width).transpose(1, 0, 2)
    adjusted_block = lax.all_to_all(by_target, "col", split_axis=0, concat_axis=0, tiled=True)
    adjusted_block = adjusted_block.reshape(ncol * height, width)
    difference = (adjusted_block.astype(jnp.float32) - base_weight.astype(jnp.float32)).astype(
        jnp.bfloat16
    )
    range_part = jnp.dot(difference, range_test, preferred_element_type=jnp.float32)
    range_chunk = scatter_sum(range_part, "col", ncol)
    range_sketch = gather_rows(range_chunk, "col", ncol)
    corange_part = jnp.dot(corange_test, difference, preferred_element_type=jnp.float32)
    corange_sketch = lax.psum(corange_part, "row")
    left_float = core_left.astype(jnp.float32)
    projected_part = jnp.dot(left_float, range_part, precision=highest)
    every = ("row", "col")
    projected = gather_rows(scatter_sum(projected_part, every, nrow * ncol), every, nrow * ncol)
    left_product = jnp.dot(core_left, difference, preferred_element_type=jnp.float32)
    partial_value = jnp.dot(left_product, core_right.astype(jnp.float32).T, precision=highest)
    own_columns = lax.psum_scatter(partial_value, "col", scatter_dimension=1, tiled=True)
    own_columns = gather_rows(scatter_sum(own_columns, "row", nrow), "row", nrow)
    gram_matrix = jnp.dot(projected.T, projected, precision=highest)
    right_hand = jnp.dot(projected.T, own_columns, precision=highest)
    factor = jnp.linalg.cholesky(gram_matrix)
    halfway = lax.linalg.triangular_solve(factor, right_hand, left_side=True, lower=True)
    core_solution = lax.linalg.triangular_solve(
        factor, halfway, left_side=True, lower=True, transpose_a=True
    )
    return (range_sketch, corange_sketch, core_solution)


def solution(mesh):
    in_specs = (
        P(("row", "col"), None),
        P("row", "col"),
        P("col", None),
        P(None, "row"),
        P(None, "row"),
        P(None, "col"),
    )
    out_specs = (P("row", None), P(None, "col"), P(None, "col"))
    return jax.shard_map(local, mesh=mesh, in_specs=in_specs, out_specs=out_specs, check_vma=False)
```

profile of v0, /device:TPU:0, one launch (start us, length us, event | category | flops | bytes accessed | tf_op | source)
XLA Modules:
  0.0 337.2 jit_solution(10886499644068481350)
XLA Ops:
  8.0 8.6 %reshape.71 = bf16[64,16,1848]{2,1,0:T(8,128)(2,1)} reshape(bf16[64,29568]{1,0:T(8,128)(2,1)} %param.6) | data formatting | bytes 7569408 | tf_op jit(solution)/shard_map/reshape | solution.py:27
  16.6 4.8 %copy.39 = bf16[64,16,1848]{2,0,1:T(8,128)(2,1)} copy(bf16[64,16,1848]{2,1,0:T(8,128)(2,1)} %reshape.71) | data formatting | bytes 7569408 | tf_op jit(solution)/shard_map/reshape | solution.py:27
  21.5 7.4 %all-to-all-start = ((bf16[16,64,1848]{2,1,0:T(8,128)(2,1)}), bf16[16,64,1848]{2,1,0:T(8,128)(2,1)}, u32[]{:S(2)}, u32[]{:S(2)}) async-start(bf16[16,64,1848]{2,1,0:T(8,128)(2,1)} %bitcast.76), calls=%async_computation | async-start | bytes 7864320 | tf_op jit(solution)/shard_map/all_to_all | solution.py:28
  28.8 6.2 %copy.27 = bf16[1024,1848]{1,0:T(8,128)(2,1)} copy(bf16[1024,1848]{0,1:T(8,128)(2,1)} %param.7) | data formatting | bytes 7569408 | tf_op args[1]
  35.1 42.8 %all-to-all-done = bf16[16,64,1848]{2,1,0:T(8,128)(2,1)} async-done(((bf16[16,64,1848]{2,1,0:T(8,128)(2,1)}), bf16[16,64,1848]{2,1,0:T(8,128)(2,1)}, u32[]{:S(2)}, u32[]{:S(2)}) %all-to-all-start) | async-done | bytes 3784736 | tf_op jit(solution)/shard_map/all_to_all | solution.py:28
  85.6 5.9 %fusion.31 = f32[1848,768]{1,0:T(8,128)} fusion(bf16[1024,1848]{1,0:T(8,128)(2,1)S(1)} %fusion, bf16[768,1024]{1,0:T(8,128)(2,1)S(1)} %copy-done.5), kind=kOutput, calls=%fused_computation.66 | convolution fusion | flops 2906652672 | bytes 11034624 | tf_op jit(solution)/shard_map/dot_general | solution.py:42
  91.6 6.3 %convolution_bitcast_fusion.1 = f32[768,384]{0,1:T(8,128)} fusion(f32[1024,384]{1,0:T(8,128)} %fusion.30, bf16[768,1024]{1,0:T(8,128)(2,1)S(1)} %copy-done.5), kind=kOutput, calls=%fused_computation.6 | convolution fusion | flops 3623878656 | bytes 4325376 | tf_op jit(solution)/shard_map/dot_general | solution.py:39
  103.0 7.6 %all-to-all-start.3 = ((f32[128,6,384]{2,1,0:T(8,128)}), f32[128,6,384]{2,1,0:T(8,128)}, u32[]{:S(2)}, u32[]{:S(2)}) async-start(f32[128,6,384]{2,1,0:T(8,128)} %all_to_all.44), calls=%async_computation.3 | async-start | bytes 3145728 | tf_op jit(solution)/shard_map/all_to_all | solution.py:11
  111.1 12.8 %fusion.32 = f32[768,768]{0,1:T(8,128)} fusion(f32[1848,768]{1,0:T(8,128)} %fusion.31, bf16[768,1848]{0,1:T(8,128)(2,1)S(1)} %copy-done), kind=kOutput, calls=%fused_computation.67 | convolution fusion | flops 13079937024 | bytes 10874880 | tf_op jit(solution)/shard_map/dot_general | solution.py:43
  123.9 9.7 %all-to-all-done.3 = f32[128,6,384]{2,1,0:T(8,128)} async-done(((f32[128,6,384]{2,1,0:T(8,128)}), f32[128,6,384]{2,1,0:T(8,128)}, u32[]{:S(2)}, u32[]{:S(2)}) %all-to-all-start.3) | async-done | bytes 1179680 | tf_op jit(solution)/shard_map/all_to_all | solution.py:11
  133.6 4.5 %all-to-all-start.1 = ((f32[16,64,384]{2,1,0:T(8,128)}), f32[16,64,384]{2,1,0:T(8,128)S(1)}, u32[]{:S(2)}, u32[]{:S(2)}) async-start(f32[16,64,384]{2,1,0:T(8,128)} %bitcast.2), calls=%async_computation.1 | async-start | bytes 3145728 | tf_op jit(solution)/shard_map/all_to_all | solution.py:11
  139.8 22.1 %all-to-all-done.1 = f32[16,64,384]{2,1,0:T(8,128)S(1)} async-done(((f32[16,64,384]{2,1,0:T(8,128)}), f32[16,64,384]{2,1,0:T(8,128)S(1)}, u32[]{:S(2)}, u32[]{:S(2)}) %all-to-all-start.1) | async-done | bytes 1572896 | tf_op jit(solution)/shard_map/all_to_all | solution.py:11
  163.5 4.6 %all-to-all-start.4 = ((f32[128,6,384]{2,1,0:T(8,128)}), f32[128,6,384]{2,1,0:T(8,128)S(1)}, u32[]{:S(2)}, u32[]{:S(2)}) async-start(f32[128,6,384]{2,1,0:T(8,128)} %broadcast_in_dim.8), calls=%async_computation.4 | async-start | bytes 3145728 | tf_op jit(solution)/shard_map/all_to_all | solution.py:19
  168.2 6.0 %convolution_bitcast_fusion = f32[384,1848]{0,1:T(8,128)} fusion(bf16[1024,1848]{1,0:T(8,128)(2,1)} %copy-done.3, bf16[384,1024]{1,0:T(8,128)(2,1)S(1)} %copy-done.8), kind=kOutput, calls=%fused_computation.5 | convolution fusion | flops 1453326336 | bytes 7409664 | tf_op jit(solution)/shard_map/dot_general | solution.py:36
  175.8 18.3 %all-to-all-done.4 = f32[128,6,384]{2,1,0:T(8,128)S(1)} async-done(((f32[128,6,384]{2,1,0:T(8,128)}), f32[128,6,384]{2,1,0:T(8,128)S(1)}, u32[]{:S(2)}, u32[]{:S(2)}) %all-to-all-start.4) | async-done | bytes 1179680 | tf_op jit(solution)/shard_map/all_to_all | solution.py:19
  196.5 11.7 %cholesky.77 = f32[128,128]{1,0:T(8,128)S(1)} custom-call(f32[128,128]{1,0:T(8,128)S(1)} %cholesky.192), custom_call_target="Cholesky" | custom-call | tf_op jit(solution)/shard_map/jit(cholesky)/cholesky | solution.py:48
  208.3 9.8 %custom-call.24 = f32[1,128,128]{1,2,0:T(8,128)S(1)} custom-call(f32[1,128,128]{2,1,0:T(8,128)S(1)} %get-tuple-element.27), custom_call_target="InvertDiagBlocksLowerTriangular" | custom-call | tf_op jit(solution)/shard_map/jit(cholesky)/cholesky | solution.py:48
  223.6 6.6 %all-to-all-done.5 = f32[8,96,48]{1,2,0:T(8,128)S(1)} async-done(((f32[8,96,48]{1,2,0:T(8,128)}), f32[8,96,48]{1,2,0:T(8,128)S(1)}, u32[]{:S(2)}, u32[]{:S(2)}) %all-to-all-start.5) | async-done | bytes 147488 | tf_op jit(solution)/shard_map/all_to_all | solution.py:11
  231.5 4.6 %all-to-all-start.2 = ((f32[16,64,384]{2,1,0:T(8,128)}), f32[16,64,384]{2,1,0:T(8,128)}, u32[]{:S(2)}, u32[]{:S(2)}) async-start(f32[16,64,384]{2,1,0:T(8,128)} %broadcast_in_dim.7), calls=%async_computation.2 | async-start | bytes 3145728 | tf_op jit(solution)/shard_map/all_to_all | solution.py:19
  236.4 11.7 %cholesky.162 = f32[128,128]{1,0:T(8,128)S(1)} custom-call(f32[128,128]{1,0:T(8,128)S(1)} %cholesky.196), custom_call_target="Cholesky" | custom-call | tf_op jit(solution)/shard_map/jit(cholesky)/cholesky | solution.py:48
  248.1 9.8 %custom-call.25 = f32[1,128,128]{1,2,0:T(8,128)S(1)} custom-call(f32[1,128,128]{2,1,0:T(8,128)S(1)} %get-tuple-element.24), custom_call_target="InvertDiagBlocksLowerTriangular" | custom-call | tf_op jit(solution)/shard_map/jit(cholesky)/cholesky | solution.py:48
  258.4 11.7 %cholesky.181 = f32[128,128]{1,0:T(8,128)S(1)} custom-call(f32[128,128]{1,0:T(8,128)S(1)} %convolution_subtract_fusion.1), custom_call_target="Cholesky" | custom-call | tf_op jit(solution)/shard_map/jit(cholesky)/cholesky | solution.py:48
  280.6 7.9 %while.1 = (s32[]{:T(128)}, f32[384,384]{1,0:T(8,128)S(1)}, s32[3,2]{0,1:T(2,128)S(1)}, f32[3,128,128]{2,1,0:T(8,128)}, s32[]{:T(128)}) while((s32[]{:T(128)}, f32[384,384]{1,0:T(8,128)S(1)}, s32[3,2]{0,1:T(2,128)S(1)}, f32[3,128,128]{2,1,0:T(8,128)}, s32[]{:T(128)}) %tuple.29), condition=%wide.while_cond, body=%wide.while_body.sunk | while | flops 2 | bytes 132705 | solution.py:50
  288.5 30.9 %custom-call.26 = f32[3,128,128]{1,2,0:T(8,128)} custom-call(f32[3,128,128]{2,1,0:T(8,128)} %get-tuple-element.10), custom_call_target="InvertDiagBlocksLowerTriangular" | custom-call | tf_op jit(solution)/shard_map/triangular_solve | solution.py:50
  (85 shorter events, 54.6 us)
Async XLA Ops:
  8.0 103.1 %copy-start = (bf16[768,1848]{0,1:T(8,128)(2,1)S(1)}, bf16[768,1848]{0,1:T(8,128)(2,1)}, u32[]{:S(2)}) copy-start(bf16[768,1848]{0,1:T(8,128)(2,1)} %param.11) | copy-start | bytes 8515588
  21.5 56.4 %all-to-all-start = ((bf16[16,64,1848]{2,1,0:T(8,128)(2,1)}), bf16[16,64,1848]{2,1,0:T(8,128)(2,1)}, u32[]{:S(2)}, u32[]{:S(2)}) async-start(bf16[16,64,1848]{2,1,0:T(8,128)(2,1)} %bitcast.76), calls=%async_computation | async-start | bytes 7864320 | tf_op jit(solution)/shard_map/all_to_all | solution.py:28
  77.8 4.4 %copy-start.7 = (bf16[1848,384]{1,0:T(8,128)(2,1)S(1)}, bf16[1848,384]{1,0:T(8,128)(2,1)}, u32[]{:S(2)}) copy-start(bf16[1848,384]{1,0:T(8,128)(2,1)} %param.8) | copy-start | bytes 4257796
  82.2 3.4 %copy-start.3 = (bf16[1024,1848]{1,0:T(8,128)(2,1)}, bf16[1024,1848]{1,0:T(8,128)(2,1)S(1)}, u32[]{:S(2)}) copy-start(bf16[1024,1848]{1,0:T(8,128)(2,1)S(1)} %fusion) | copy-start | bytes 11354116
  82.2 3.4 %copy-start.5 = (bf16[768,1024]{1,0:T(8,128)(2,1)S(1)}, bf16[768,1024]{1,0:T(8,128)(2,1)}, u32[]{:S(2)}) copy-start(bf16[768,1024]{1,0:T(8,128)(2,1)} %param.10) | copy-start | bytes 4718596
  103.0 30.6 %all-to-all-start.3 = ((f32[128,6,384]{2,1,0:T(8,128)}), f32[128,6,384]{2,1,0:T(8,128)}, u32[]{:S(2)}, u32[]{:S(2)}) async-start(f32[128,6,384]{2,1,0:T(8,128)} %all_to_all.44), calls=%async_computation.3 | async-start | bytes 3145728 | tf_op jit(solution)/shard_map/all_to_all | solution.py:11
  110.6 107.5 %reduce-scatter.2.cloned.1.call-start = ((), (), s32[]{:S(2)}) async-start(), calls=%async_computation.9 | async-start | bytes 2506752 | tf_op jit(solution)/shard_map/reduce_scatter | solution.py:44
  133.6 28.2 %all-to-all-start.1 = ((f32[16,64,384]{2,1,0:T(8,128)}), f32[16,64,384]{2,1,0:T(8,128)S(1)}, u32[]{:S(2)}, u32[]{:S(2)}) async-start(f32[16,64,384]{2,1,0:T(8,128)} %bitcast.2), calls=%async_computation.1 | async-start | bytes 3145728 | tf_op jit(solution)/shard_map/all_to_all | solution.py:11
  139.7 28.5 %copy-start.8 = (bf16[384,1024]{1,0:T(8,128)(2,1)S(1)}, bf16[384,1024]{1,0:T(8,128)(2,1)}, u32[]{:S(2)}) copy-start(bf16[384,1024]{1,0:T(8,128)(2,1)} %param.9) | copy-start | bytes 2359300
  161.8 1.7 copy-start.2
  163.5 30.6 %all-to-all-start.4 = ((f32[128,6,384]{2,1,0:T(8,128)}), f32[128,6,384]{2,1,0:T(8,128)S(1)}, u32[]{:S(2)}, u32[]{:S(2)}) async-start(f32[128,6,384]{2,1,0:T(8,128)} %broadcast_in_dim.8), calls=%async_computation.4 | async-start | bytes 3145728 | tf_op jit(solution)/shard_map/all_to_all | solution.py:19
  168.2 157.0 %all-reduce.3.cloned.1.call-start = ((), (), s32[]{:S(2)}) async-start(), calls=%async_computation.8 | async-start | bytes 5677056 | tf_op jit(solution)/shard_map/psum | solution.py:37
  219.9 10.3 %all-to-all-start.5 = ((f32[8,96,48]{1,2,0:T(8,128)}), f32[8,96,48]{1,2,0:T(8,128)S(1)}, u32[]{:S(2)}, u32[]{:S(2)}) async-start(f32[8,96,48]{1,2,0:T(8,128)} %copy.32), calls=%async_computation.6 | async-start | bytes 393216 | tf_op jit(solution)/shard_map/all_to_all | solution.py:11
  231.5 44.0 %all-to-all-start.2 = ((f32[16,64,384]{2,1,0:T(8,128)}), f32[16,64,384]{2,1,0:T(8,128)}, u32[]{:S(2)}, u32[]{:S(2)}) async-start(f32[16,64,384]{2,1,0:T(8,128)} %broadcast_in_dim.7), calls=%async_computation.2 | async-start | bytes 3145728 | tf_op jit(solution)/shard_map/all_to_all | solution.py:19
  276.2 43.4 %all-to-all-start.6 = ((f32[8,96,48]{1,2,0:T(8,128)}), f32[8,96,48]{1,2,0:T(8,128)}, u32[]{:S(2)}, u32[]{:S(2)}) async-start(f32[8,96,48]{1,2,0:T(8,128)} %broadcast_in_dim.9), calls=%async_computation.7 | async-start | bytes 393216 | tf_op jit(solution)/shard_map/all_to_all | solution.py:19
  319.6 3.2 copy-start.6
  325.1 2.8 copy-start.4
  325.1 4.4 %copy-start.1 = (bf16[768,1848]{0,1:T(8,128)(2,1)S(1)}, bf16[768,1848]{0,1:T(8,128)(2,1)}, u32[]{:S(2)}) copy-start(bf16[768,1848]{0,1:T(8,128)(2,1)} %param.11) | copy-start | bytes 8515588
Sparse Core Ops, SparseCore 0:
  124.0 87.1 reduce-scatter.1
Sparse Core Ops, SparseCore 1:
  174.3 107.9 all-reduce.2
where the time goes:
time: 342 us; the launch traced here: 337 us
  waiting for transfers between devices  101 us (30%)
  other arithmetic  95.5 us (28%)
  local copies, waits for them, and re-layouts  44 us (13%)
  matrix products  41.3 us (12%)
  starting transfers between devices  36.9 us (11%)
  between operations  18 us (5%)
    another operation x10, other arithmetic, local(): factor = jnp.linalg.cholesky(gram_matrix)  56.3 us
    all_to_all x1, waiting for transfers between devices, local(): lax.all_to_all(by_target, 'col', split_axis=0, concat_axis=0, tiled=True)  42.8 us
    all_to_all x3, waiting for transfers between devices, scatter_sum(): got = lax.all_to_all(part, axis, split_axis=0, concat_axis=0, tiled=True)  38.4 us
    another operation x4, other arithmetic, local(): lax.linalg.triangular_solve(factor, halfway, left_side=True, lower=True,...  31.6 us
    all_to_all x3, waiting for transfers between devices, gather_rows(): return lax.all_to_all(tiled, axis, split_axis=0, concat_axis=0, tiled=True)  20.2 us
    all_to_all x3, starting transfers between devices, scatter_sum(): got = lax.all_to_all(part, axis, split_axis=0, concat_axis=0, tiled=True)  15.5 us
    all_to_all x3, starting transfers between devices, gather_rows(): return lax.all_to_all(tiled, axis, split_axis=0, concat_axis=0, tiled=True)  13.5 us
    reshape x2, local copies, waits for them, and re-layouts, local(): by_target = adjusted_rows.reshape(height, ncol, width).transpose(1, 0, 2)  13.4 us
  transfers between devices with their start and end apart: 9, of which 6 were waited for; matrix products, arithmetic and copies ran while one was open for 40% of the time, Pallas kernels for 0%

commit v1 on v0

--- a/solution.py
+++ b/solution.py
@@ -31,10 +31,7 @@
         jnp.bfloat16
     )
     range_part = jnp.dot(difference, range_test, preferred_element_type=jnp.float32)
-    range_chunk = scatter_sum(range_part, "col", ncol)
-    range_sketch = gather_rows(range_chunk, "col", ncol)
     corange_part = jnp.dot(corange_test, difference, preferred_element_type=jnp.float32)
-    corange_sketch = lax.psum(corange_part, "row")
     left_float = core_left.astype(jnp.float32)
     projected_part = jnp.dot(left_float, range_part, precision=highest)
     every = ("row", "col")
@@ -42,6 +39,11 @@
     left_product = jnp.dot(core_left, difference, preferred_element_type=jnp.float32)
     partial_value = jnp.dot(left_product, core_right.astype(jnp.float32).T, precision=highest)
     own_columns = lax.psum_scatter(partial_value, "col", scatter_dimension=1, tiled=True)
+    projected, range_part, corange_part = lax.optimization_barrier(
+        (projected, range_part, corange_part)
+    )
+    range_sketch = gather_rows(scatter_sum(range_part, "col", ncol), "col", ncol)
+    corange_sketch = gather_rows(scatter_sum(corange_part, "row", nrow), "row", nrow)
     own_columns = gather_rows(scatter_sum(own_columns, "row", nrow), "row", nrow)
     gram_matrix = jnp.dot(projected.T, projected, precision=highest)
     right_hand = jnp.dot(projected.T, own_columns, precision=highest)

time: 342 us -> 442 us (1.29)
  waiting for transfers between devices: 101 us -> 176 us
  local copies, waits for them, and re-layouts: 44 us -> 53.8 us
  starting transfers between devices: 36.9 us -> 46.5 us
    reduce_scatter x1, waiting for transfers between devices: 0.02 us -> 56.1 us  [local(): lax.psum_scatter(partial_value, 'col', scatter_dimension=1, tiled=True)]
    all_to_all x3 -> x4, waiting for transfers between devices: 20.2 us -> 50.9 us  [gather_rows(): return lax.all_to_all(tiled, axis, split_axis=0, concat_axis=0, tiled=True)]
    all_to_all x3 -> x4, waiting for transfers between devices: 38.4 us -> 26.9 us  [scatter_sum(): got = lax.all_to_all(part, axis, split_axis=0, concat_axis=0, tiled=True)]
    all_to_all x3 -> x4, starting transfers between devices: 13.5 us -> 18.8 us  [gather_rows(): return lax.all_to_all(tiled, axis, split_axis=0, concat_axis=0, tiled=True)]
    all_to_all x3 -> x4, starting transfers between devices: 15.5 us -> 20.5 us  [scatter_sum(): got = lax.all_to_all(part, axis, split_axis=0, concat_axis=0, tiled=True)]
    unnamed x21 -> x25, local copies, waits for them, and re-layouts: 10.9 us -> 14.3 us
  transfers between devices with their start and end apart: 9 -> 10, of which waited for: 6 -> 7; matrix products, arithmetic and copies ran while one was open for 40% -> 34% of each run, Pallas kernels for 0% -> 0%
where the time goes in v1:
time: 442 us; the launch traced here: 436 us
  waiting for transfers between devices  176 us (40%)
  other arithmetic  97.7 us (22%)
  local copies, waits for them, and re-layouts  53.8 us (12%)
  starting transfers between devices  46.5 us (11%)
  matrix products  45.6 us (10%)
  between operations  16.6 us (4%)
    another operation x10, other arithmetic, local(): factor = jnp.linalg.cholesky(gram_matrix)  56.4 us
    reduce_scatter x1, waiting for transfers between devices, local(): lax.psum_scatter(partial_value, 'col', scatter_dimension=1, tiled=True)  56.1 us
    all_to_all x4, waiting for transfers between devices, gather_rows(): return lax.all_to_all(tiled, axis, split_axis=0, concat_axis=0, tiled=True)  50.9 us
    all_to_all x1, waiting for transfers between devices, local(): lax.all_to_all(by_target, 'col', split_axis=0, concat_axis=0, tiled=True)  42.4 us
    another operation x4, other arithmetic, local(): lax.linalg.triangular_solve(factor, halfway, left_side=True, lower=True,...  32.7 us
    all_to_all x4, waiting for transfers between devices, scatter_sum(): got = lax.all_to_all(part, axis, split_axis=0, concat_axis=0, tiled=True)  26.9 us
    all_to_all x4, starting transfers between devices, scatter_sum(): got = lax.all_to_all(part, axis, split_axis=0, concat_axis=0, tiled=True)  20.5 us
    all_to_all x4, starting transfers between devices, gather_rows(): return lax.all_to_all(tiled, axis, split_axis=0, concat_axis=0, tiled=True)  18.8 us
  transfers between devices with their start and end apart: 10, of which 7 were waited for; matrix products, arithmetic and copies ran while one was open for 34% of the time, Pallas kernels for 0%

profile of v1, /device:TPU:0, one launch (start us, length us, event | category | flops | bytes accessed | tf_op | source)
XLA Modules:
  0.0 436.5 jit_solution(1724328130812449578)
XLA Ops:
  7.2 8.6 %reshape.80 = bf16[64,16,1848]{2,1,0:T(8,128)(2,1)} reshape(bf16[64,29568]{1,0:T(8,128)(2,1)} %param.6) | data formatting | bytes 7569408 | tf_op jit(solution)/shard_map/reshape | solution.py:27
  15.8 4.9 %copy.36 = bf16[64,16,1848]{2,0,1:T(8,128)(2,1)} copy(bf16[64,16,1848]{2,1,0:T(8,128)(2,1)} %reshape.80) | data formatting | bytes 7569408 | tf_op jit(solution)/shard_map/reshape | solution.py:27
  20.6 7.2 %all-to-all-start = ((bf16[16,64,1848]{2,1,0:T(8,128)(2,1)}), bf16[16,64,1848]{2,1,0:T(8,128)(2,1)}, u32[]{:S(2)}, u32[]{:S(2)}) async-start(bf16[16,64,1848]{2,1,0:T(8,128)(2,1)} %bitcast.78), calls=%async_computation | async-start | bytes 7864320 | tf_op jit(solution)/shard_map/all_to_all | solution.py:28
  27.9 6.6 %copy.26 = bf16[1024,1848]{1,0:T(8,128)(2,1)} copy(bf16[1024,1848]{0,1:T(8,128)(2,1)} %param.7) | data formatting | bytes 7569408 | tf_op args[1]
  34.5 42.4 %all-to-all-done = bf16[16,64,1848]{2,1,0:T(8,128)(2,1)} async-done(((bf16[16,64,1848]{2,1,0:T(8,128)(2,1)}), bf16[16,64,1848]{2,1,0:T(8,128)(2,1)}, u32[]{:S(2)}, u32[]{:S(2)}) %all-to-all-start) | async-done | bytes 3784736 | tf_op jit(solution)/shard_map/all_to_all | solution.py:28
  84.6 9.6 %fusion.32 = f32[768,768]{0,1:T(8,128)} fusion(f32[1848,768]{1,0:T(8,128)S(1)} %fusion.31, bf16[768,1848]{0,1:T(8,128)(2,1)S(1)} %copy-done), kind=kOutput, calls=%fused_computation.66 | convolution fusion | flops 13079937024 | bytes 10874880 | tf_op jit(solution)/shard_map/dot_general | solution.py:40
  94.3 6.0 %fusion.29 = f32[1024,384]{1,0:T(8,128)} fusion(bf16[1024,1848]{1,0:T(8,128)(2,1)} %copy-done.3, bf16[1848,384]{1,0:T(8,128)(2,1)} %param.8), kind=kOutput, calls=%fused_computation.63 | convolution fusion | flops 1453326336 | bytes 6776832 | tf_op jit(solution)/shard_map/dot_general | solution.py:33
  100.3 5.3 %convolution_bitcast_fusion.1 = f32[768,384]{0,1:T(8,128)S(1)} fusion(f32[1024,384]{1,0:T(8,128)} %fusion.29, bf16[768,1024]{1,0:T(8,128)(2,1)S(1)} %copy-done.7), kind=kOutput, calls=%fused_computation.6 | convolution fusion | flops 3623878656 | bytes 4325376 | tf_op jit(solution)/shard_map/dot_general | solution.py:36
  107.3 7.1 %all-to-all-start.1 = ((f32[128,6,384]{2,1,0:T(8,128)}), f32[128,6,384]{2,1,0:T(8,128)S(1)}, u32[]{:S(2)}, u32[]{:S(2)}) async-start(f32[128,6,384]{2,1,0:T(8,128)} %all_to_all.52), calls=%async_computation.1 | async-start | bytes 3145728 | tf_op jit(solution)/shard_map/all_to_all | solution.py:11
  114.5 56.1 %reduce-scatter.2.cloned.1.call-done = f32[768,48]{0,1:T(8,128)} async-done(((f32[768,768]{0,1:T(8,128)}), f32[768,48]{0,1:T(8,128)}) %reduce-scatter.2.cloned.1.call-update) | async-done | bytes 147472 | tf_op jit(solution)/shard_map/reduce_scatter | solution.py:41
  177.1 6.8 %all-to-all-done.7 = f32[8,96,48]{1,2,0:T(8,128)S(1)} async-done(((f32[8,96,48]{1,2,0:T(8,128)}), f32[8,96,48]{1,2,0:T(8,128)S(1)}, u32[]{:S(2)}, u32[]{:S(2)}) %all-to-all-start.7) | async-done | bytes 147488 | tf_op jit(solution)/shard_map/all_to_all | solution.py:11
  185.1 6.1 %all-to-all-start.2 = ((f32[128,6,384]{2,1,0:T(8,128)}), f32[128,6,384]{2,1,0:T(8,128)S(1)}, u32[]{:S(2)}, u32[]{:S(2)}) async-start(f32[128,6,384]{2,1,0:T(8,128)} %broadcast_in_dim.9), calls=%async_computation.2 | async-start | bytes 3145728 | tf_op jit(solution)/shard_map/all_to_all | solution.py:19
  191.2 23.3 %all-to-all-done.2 = f32[128,6,384]{2,1,0:T(8,128)S(1)} async-done(((f32[128,6,384]{2,1,0:T(8,128)}), f32[128,6,384]{2,1,0:T(8,128)S(1)}, u32[]{:S(2)}, u32[]{:S(2)}) %all-to-all-start.2) | async-done | bytes 1179680 | tf_op jit(solution)/shard_map/all_to_all | solution.py:19
  218.7 5.9 %convolution_bitcast_fusion = f32[384,1848]{0,1:T(8,128)} fusion(bf16[1024,1848]{1,0:T(8,128)(2,1)} %copy-done.3, bf16[384,1024]{1,0:T(8,128)(2,1)S(1)} %copy-done.10), kind=kOutput, calls=%fused_computation.5 | convolution fusion | flops 1453326336 | bytes 7409664 | tf_op jit(solution)/shard_map/dot_general | solution.py:34
  233.6 20.1 %all-to-all-done.3 = f32[16,64,384]{2,1,0:T(8,128)S(1)} async-done(((f32[16,64,384]{2,1,0:T(8,128)}), f32[16,64,384]{2,1,0:T(8,128)S(1)}, u32[]{:S(2)}, u32[]{:S(2)}) %all-to-all-start.3) | async-done | bytes 1572896 | tf_op jit(solution)/shard_map/all_to_all | solution.py:11
  263.7 11.7 %cholesky.77 = f32[128,128]{1,0:T(8,128)S(1)} custom-call(f32[128,128]{1,0:T(8,128)S(1)} %cholesky.192), custom_call_target="Cholesky" | custom-call | tf_op jit(solution)/shard_map/jit(cholesky)/cholesky | solution.py:50
  275.5 9.8 %custom-call.24 = f32[1,128,128]{1,2,0:T(8,128)S(1)} custom-call(f32[1,128,128]{2,1,0:T(8,128)S(1)} %get-tuple-element.42), custom_call_target="InvertDiagBlocksLowerTriangular" | custom-call | tf_op jit(solution)/shard_map/jit(cholesky)/cholesky | solution.py:50
  288.3 11.8 %cholesky.162 = f32[128,128]{1,0:T(8,128)S(1)} custom-call(f32[128,128]{1,0:T(8,128)S(1)} %cholesky.196), custom_call_target="Cholesky" | custom-call | tf_op jit(solution)/shard_map/jit(cholesky)/cholesky | solution.py:50
  300.2 9.8 %custom-call.25 = f32[1,128,128]{1,2,0:T(8,128)S(1)} custom-call(f32[1,128,128]{2,1,0:T(8,128)S(1)} %get-tuple-element.39), custom_call_target="InvertDiagBlocksLowerTriangular" | custom-call | tf_op jit(solution)/shard_map/jit(cholesky)/cholesky | solution.py:50
  312.2 11.7 %cholesky.181 = f32[128,128]{1,0:T(8,128)S(1)} custom-call(f32[128,128]{1,0:T(8,128)S(1)} %convolution_subtract_fusion.1), custom_call_target="Cholesky" | custom-call | tf_op jit(solution)/shard_map/jit(cholesky)/cholesky | solution.py:50
  333.6 8.2 %while.1 = (s32[]{:T(128)}, f32[384,384]{1,0:T(8,128)S(1)}, s32[3,2]{0,1:T(2,128)S(1)}, f32[3,128,128]{2,1,0:T(8,128)}, s32[]{:T(128)}) while((s32[]{:T(128)}, f32[384,384]{1,0:T(8,128)S(1)}, s32[3,2]{0,1:T(2,128)S(1)}, f32[3,128,128]{2,1,0:T(8,128)}, s32[]{:T(128)}) %tuple.34), condition=%wide.while_cond, body=%wide.while_body.sunk | while | flops 2 | bytes 132205 | solution.py:52
  341.8 30.9 %custom-call.26 = f32[3,128,128]{1,2,0:T(8,128)} custom-call(f32[3,128,128]{2,1,0:T(8,128)} %get-tuple-element.16), custom_call_target="InvertDiagBlocksLowerTriangular" | custom-call | tf_op jit(solution)/shard_map/triangular_solve | solution.py:52
  381.9 5.6 %all-to-all-start.6 = ((f32[8,48,1848]{2,1,0:T(8,128)}), f32[8,48,1848]{2,1,0:T(8,128)}, u32[]{:S(2)}, u32[]{:S(2)}) async-start(f32[8,48,1848]{2,1,0:T(8,128)} %broadcast_in_dim.11), calls=%async_computation.6 | async-start | bytes 5898240 | tf_op jit(solution)/shard_map/all_to_all | solution.py:19
  397.0 26.2 %all-to-all-done.6 = f32[8,48,1848]{2,1,0:T(8,128)} async-done(((f32[8,48,1848]{2,1,0:T(8,128)}), f32[8,48,1848]{2,1,0:T(8,128)}, u32[]{:S(2)}, u32[]{:S(2)}) %all-to-all-start.6) | async-done | bytes 2838560 | tf_op jit(solution)/shard_map/all_to_all | solution.py:19
  (93 shorter events, 86.3 us)
Async XLA Ops:
  7.2 77.5 %copy-start = (bf16[768,1848]{0,1:T(8,128)(2,1)S(1)}, bf16[768,1848]{0,1:T(8,128)(2,1)}, u32[]{:S(2)}) copy-start(bf16[768,1848]{0,1:T(8,128)(2,1)} %param.11) | copy-start | bytes 8515588
  20.6 56.2 %all-to-all-start = ((bf16[16,64,1848]{2,1,0:T(8,128)(2,1)}), bf16[16,64,1848]{2,1,0:T(8,128)(2,1)}, u32[]{:S(2)}, u32[]{:S(2)}) async-start(bf16[16,64,1848]{2,1,0:T(8,128)(2,1)} %bitcast.78), calls=%async_computation | async-start | bytes 7864320 | tf_op jit(solution)/shard_map/all_to_all | solution.py:28
  27.8 142.7 %reduce-scatter.2.cloned.1.call-start = ((), (), s32[]{:S(2)}) async-start(), calls=%async_computation.10 | async-start | bytes 2506752 | tf_op jit(solution)/shard_map/reduce_scatter | solution.py:41
  76.8 4.4 %copy-start.6 = (bf16[768,1024]{1,0:T(8,128)(2,1)S(1)}, bf16[768,1024]{1,0:T(8,128)(2,1)}, u32[]{:S(2)}) copy-start(bf16[768,1024]{1,0:T(8,128)(2,1)} %param.10) | copy-start | bytes 4718596
  81.2 3.4 copy-start.3
  94.3 6.1 %copy-start.7 = (bf16[768,1024]{1,0:T(8,128)(2,1)S(1)}, bf16[768,1024]{1,0:T(8,128)(2,1)}, u32[]{:S(2)}) copy-start(bf16[768,1024]{1,0:T(8,128)(2,1)} %param.10) | copy-start | bytes 4718596
  107.3 65.0 %all-to-all-start.1 = ((f32[128,6,384]{2,1,0:T(8,128)}), f32[128,6,384]{2,1,0:T(8,128)S(1)}, u32[]{:S(2)}, u32[]{:S(2)}) async-start(f32[128,6,384]{2,1,0:T(8,128)} %all_to_all.52), calls=%async_computation.1 | async-start | bytes 3145728 | tf_op jit(solution)/shard_map/all_to_all | solution.py:11
  172.3 11.5 %all-to-all-start.7 = ((f32[8,96,48]{1,2,0:T(8,128)}), f32[8,96,48]{1,2,0:T(8,128)S(1)}, u32[]{:S(2)}, u32[]{:S(2)}) async-start(f32[8,96,48]{1,2,0:T(8,128)} %copy.30), calls=%async_computation.8 | async-start | bytes 393216 | tf_op jit(solution)/shard_map/all_to_all | solution.py:11
  177.1 41.6 %copy-start.10 = (bf16[384,1024]{1,0:T(8,128)(2,1)S(1)}, bf16[384,1024]{1,0:T(8,128)(2,1)}, u32[]{:S(2)}) copy-start(bf16[384,1024]{1,0:T(8,128)(2,1)} %param.9) | copy-start | bytes 2359300
  185.1 29.4 %all-to-all-start.2 = ((f32[128,6,384]{2,1,0:T(8,128)}), f32[128,6,384]{2,1,0:T(8,128)S(1)}, u32[]{:S(2)}, u32[]{:S(2)}) async-start(f32[128,6,384]{2,1,0:T(8,128)} %broadcast_in_dim.9), calls=%async_computation.2 | async-start | bytes 3145728 | tf_op jit(solution)/shard_map/all_to_all | solution.py:19
  215.2 10.9 %all-to-all-start.8 = ((f32[8,96,48]{1,2,0:T(8,128)}), f32[8,96,48]{1,2,0:T(8,128)S(1)}, u32[]{:S(2)}, u32[]{:S(2)}) async-start(f32[8,96,48]{1,2,0:T(8,128)} %broadcast_in_dim.12), calls=%async_computation.9 | async-start | bytes 393216 | tf_op jit(solution)/shard_map/all_to_all | solution.py:19
  226.1 7.5 %copy-start.8 = (f32[8,96,48]{1,2,0:T(8,128)}, f32[8,96,48]{1,2,0:T(8,128)S(1)}, u32[]{:S(2)}) copy-start(f32[8,96,48]{1,2,0:T(8,128)S(1)} %all-to-all-done.8) | copy-start | bytes 442372
  226.1 27.6 %all-to-all-start.3 = ((f32[16,64,384]{2,1,0:T(8,128)}), f32[16,64,384]{2,1,0:T(8,128)S(1)}, u32[]{:S(2)}, u32[]{:S(2)}) async-start(f32[16,64,384]{2,1,0:T(8,128)} %bitcast.4), calls=%async_computation.3 | async-start | bytes 3145728 | tf_op jit(solution)/shard_map/all_to_all | solution.py:11
  253.7 70.3 %all-to-all-start.5 = ((f32[8,48,1848]{2,1,0:T(8,128)}), f32[8,48,1848]{2,1,0:T(8,128)}, u32[]{:S(2)}, u32[]{:S(2)}) async-start(f32[8,48,1848]{2,1,0:T(8,128)} %bitcast.79), calls=%async_computation.5 | async-start | bytes 5898240 | tf_op jit(solution)/shard_map/all_to_all | solution.py:11
  262.8 0.8 copy-start.5
  287.6 0.7 copy-start.9
  323.9 1.4 copy-start.4
  325.3 53.5 %all-to-all-start.4 = ((f32[16,64,384]{2,1,0:T(8,128)}), f32[16,64,384]{2,1,0:T(8,128)S(1)}, u32[]{:S(2)}, u32[]{:S(2)}) async-start(f32[16,64,384]{2,1,0:T(8,128)} %broadcast_in_dim.10), calls=%async_computation.4 | async-start | bytes 3145728 | tf_op jit(solution)/shard_map/all_to_all | solution.py:19
  378.8 3.1 copy-start.2
  381.9 41.3 %all-to-all-start.6 = ((f32[8,48,1848]{2,1,0:T(8,128)}), f32[8,48,1848]{2,1,0:T(8,128)}, u32[]{:S(2)}, u32[]{:S(2)}) async-start(f32[8,48,1848]{2,1,0:T(8,128)} %broadcast_in_dim.11), calls=%async_computation.6 | async-start | bytes 5898240 | tf_op jit(solution)/shard_map/all_to_all | solution.py:19
  423.2 6.2 %copy-start.1 = (bf16[768,1848]{0,1:T(8,128)(2,1)S(1)}, bf16[768,1848]{0,1:T(8,128)(2,1)}, u32[]{:S(2)}) copy-start(bf16[768,1848]{0,1:T(8,128)(2,1)} %param.11) | copy-start | bytes 8515588
Sparse Core Ops, SparseCore 0:
  94.4 76.1 reduce-scatter.1
